TPU v7x, 32 devices: a whole 2x2x4 slice. The times are simulated.
32 devices in a mesh: clips: 2 (over y), tm: 4 (over x, core), rows: 4 (over z).
Axes of the slice: x: 2, y: 2, z: 4, core: 2. Of those that a mesh axis runs over, the one named last changes fastest.
Arguments:
- segment_input: bfloat16 [4, 8, 4, 32, 384], P('clips', 'tm', 'rows'), parts along dimension 0, may hold values from -6 to 6
- inner_input: bfloat16 [4, 8, 4, 32, 384], P('clips', 'tm', 'rows'), parts along dimension 0, may hold values from -6 to 6
- lengths: int32 [4, 4], P('clips', 'tm'), parts along dimension 0, may hold values from 1 to 2
- inner_gain: float32 [384], replicated, may hold values from 0.25 to 1.75
- causal_weight: bfloat16 [3, 3, 3, 384, 384], replicated, may hold values from -0.0625 to 0.0625
- causal_bias: float32 [384], replicated, may hold values from -3 to 3
- attention_gain: float32 [384], replicated, may hold values from 0.25 to 1.75
- triple_weight: bfloat16 [384, 1152], replicated, may hold values from -0.4375 to 0.4375
- triple_bias: float32 [1152], replicated, may hold values from -150 to 150
- output_weight: bfloat16 [384, 384], replicated, may hold values from -0.3125 to 0.3125
- output_bias: float32 [384], replicated, may hold values from -3 to 3
Outputs:
- encoded: bfloat16 [4, 8, 4, 32, 384], P('clips', 'tm', 'rows'), parts along dimension 0
There are 2 independent parts, one for each index of `clips`. A program takes and returns all parts, laid end to end along the dimension named above; an argument that names none is the same for every part. Nothing has to cross between parts.
Inputs may be any that keep to these rules, and one draw needn't show every extreme that they name: The valid frames of a clip in a section are that section's first lengths[b, s] frame slots.
All inputs are finite; a program needn't handle non-finite values.
Results may differ from a plain program's by a relative error of at most 0.0062.
Values may be sent and summed in bfloat16 or wider, within the bound.
No kernel may reach another device: no remote copies, remote signals or barrier semaphores. Data moves between devices by JAX's collectives and lax.ppermute only.
A program may use at most 128 MiB of HBM per device.

v0:
```python
import math
import jax
import jax.numpy as jnp
from jax import lax
from jax.sharding import PartitionSpec as P

EPSILON = 1e-06


def prefix(part, axis, combine, identity):
    place = lax.axis_index(axis)
    gathered = jax.tree.map(lambda a: lax.all_gather(a, axis), part)
    state = jax.tree.map(lambda a, e: jnp.zeros_like(a) + jnp.asarray(e, a.dtype), part, identity)

    def one(step, state):
        return combine(
            state, jax.tree.map(lambda a: lax.dynamic_index_in_dim(a, step, 0, False), gathered)
        )

    return lax.fori_loop(0, place, one, state)


def as_sent(x):

    def short(part):
        return part.astype(jnp.bfloat16) if part.dtype == jnp.float32 else part

    return jax.tree.map(short, x)


def with_halo(cells, sides, width):
    for axis, dim in sides:
        count = lax.axis_size(axis)
        ends = count - 1
        head = lax.slice_in_dim(cells, 0, width, axis=dim)
        tail = lax.slice_in_dim(cells, cells.shape[dim] - width, cells.shape[dim], axis=dim)
        cells = jnp.concatenate(
            [
                lax.ppermute(tail, axis, [(i, (i + 1) % count) for i in range(ends)]),
                cells,
                lax.ppermute(head, axis, [((i + 1) % count, i) for i in range(ends)]),
            ],
            axis=dim,
        )
    return cells


def normalize(field, gain):
    widened = field.astype(jnp.float32)
    return widened * lax.rsqrt(jnp.mean(widened * widened, axis=-1, keepdims=True) + EPSILON) * gain


def last_two(extended, counts):
    slot_total = extended.shape[1]
    chosen = []
    for position in range(2):
        target = counts + position
        picked = jnp.zeros_like(extended[:, 0])
        for slot_index in range(slot_total):
            matches = (target == slot_index)[:, None, None, None]
            picked = jnp.where(matches, extended[:, slot_index], picked)
        chosen.append(picked)
    return jnp.stack(chosen, axis=1)


def summarize(activated, counts):
    blanks = jnp.zeros((activated.shape[0], 2) + activated.shape[2:], activated.dtype)
    summary = last_two(jnp.concatenate([blanks, activated], axis=1), counts)
    return (summary, jnp.minimum(counts, 2).astype(jnp.bfloat16))


def join_later(earlier, later):
    early_frames, early_count = earlier
    late_frames, late_count = later
    complete = (late_count > 1.5)[:, None, None, None, None]
    single = (late_count > 0.5)[:, None, None, None, None]
    shifted = jnp.concatenate([early_frames[:, 1:], late_frames[:, 1:]], axis=1)
    frames = jnp.where(complete, late_frames, jnp.where(single, shifted, early_frames))
    total_count = jnp.minimum(early_count + late_count, 2.0).astype(early_count.dtype)
    return (frames, total_count)


def incoming_cache(summary, counts):
    starting = (jnp.zeros_like(summary), jnp.zeros_like(counts))
    combined = prefix((summary, counts), "tm", join_later, starting)
    return combined[0]


def convolve(padded, causal_weight, causal_bias):
    clip_count, slot_total, rows_padded, column_count, channels = padded.shape
    frame_count = slot_total - 2
    row_count = rows_padded - 2
    widened = jnp.pad(padded, ((0, 0), (0, 0), (0, 0), (1, 1), (0, 0)))
    summed = jnp.zeros((clip_count * frame_count * row_count * column_count, channels), jnp.float32)
    for delta_time in range(3):
        for delta_row in range(3):
            window = widened[
                :, delta_time : delta_time + frame_count, delta_row : delta_row + row_count
            ]
            columns = jnp.concatenate(
                [window[:, :, :, delta_col : delta_col + column_count] for delta_col in range(3)],
                axis=-1,
            )
            kernel = causal_weight[delta_time, delta_row].reshape(3 * channels, channels)
            summed = summed + jnp.dot(
                columns.reshape(-1, 3 * channels), kernel, preferred_element_type=jnp.float32
            )
    return summed.reshape(clip_count, frame_count, row_count, column_count, channels) + causal_bias


def attend(normed, triple_weight, triple_bias, output_weight, output_bias):
    frame_count, places, channels = normed.shape
    packed = (
        jnp.dot(normed.reshape(-1, channels), triple_weight, preferred_element_type=jnp.float32)
        + triple_bias
    )
    packed = packed.reshape(frame_count, places, 3 * channels)
    queries = packed[:, :, :channels]
    key_vectors = packed[:, :, channels : 2 * channels]
    values = packed[:, :, 2 * channels :].astype(jnp.bfloat16)
    scores = jnp.einsum(
        "nqc,nkc->nqk", queries, key_vectors, precision=lax.Precision.HIGHEST
    ) / math.sqrt(channels)
    row_max = jnp.max(scores, axis=-1, keepdims=True)
    exponent = jnp.exp(scores - row_max)
    weights = (exponent / jnp.sum(exponent, axis=-1, keepdims=True)).astype(jnp.bfloat16)
    attended = jnp.einsum(
        "nqk,nkc->nqc", weights, values, preferred_element_type=jnp.float32
    ).astype(jnp.bfloat16)
    projected = (
        jnp.dot(attended.reshape(-1, channels), output_weight, preferred_element_type=jnp.float32)
        + output_bias
    )
    return projected.reshape(frame_count, places, channels).astype(jnp.bfloat16)


def body(
    segment_input,
    inner_input,
    lengths,
    inner_gain,
    causal_weight,
    causal_bias,
    attention_gain,
    triple_weight,
    triple_bias,
    output_weight,
    output_bias,
):
    clip_count, frame_count, row_count, column_count, channels = segment_input.shape
    activated = jax.nn.silu(normalize(inner_input, inner_gain)).astype(jnp.bfloat16)
    counts = lengths[:, 0]
    live_mask = (jnp.arange(frame_count, dtype=jnp.int32)[None, :] < counts[:, None]).astype(
        jnp.float32
    )
    carried = incoming_cache(*summarize(activated, counts))
    extended = jnp.concatenate([carried, activated], axis=1)
    padded = with_halo(as_sent(extended), (("rows", 2),), 1).astype(extended.dtype)
    convolved = convolve(padded, causal_weight, causal_bias)
    residual = (segment_input.astype(jnp.float32) + convolved).astype(jnp.bfloat16)
    residual = lax.optimization_barrier(residual)
    normed = normalize(residual, attention_gain).astype(jnp.bfloat16)
    row_devices = lax.axis_size("rows")
    per_device = clip_count * frame_count // row_devices
    grouped = normed.reshape(row_devices, per_device, row_count, column_count, channels)
    portion = lax.all_to_all(grouped, "rows", split_axis=0, concat_axis=2, tiled=True)
    owned = portion.shape[1]
    height = portion.shape[2]
    flat = portion.reshape(owned, height * column_count, channels)
    result = attend(flat, triple_weight, triple_bias, output_weight, output_bias)
    result = result.reshape(1, owned, height, column_count, channels)
    projected = lax.all_to_all(result, "rows", split_axis=2, concat_axis=0, tiled=True)
    projected = projected.reshape(clip_count, frame_count, row_count, column_count, channels)
    projected = lax.optimization_barrier(projected)
    summed = residual.astype(jnp.float32) + projected.astype(jnp.float32)
    return (summed * live_mask[:, :, None, None, None]).astype(jnp.bfloat16)


def activate(field, gain):
    return jax.nn.silu(normalize(field, gain)).astype(jnp.bfloat16)


def conv3d(frames, causal_weight, time_padding):
    return lax.conv_general_dilated(
        frames,
        causal_weight,
        window_strides=(1, 1, 1),
        padding=(time_padding, (1, 1), (1, 1)),
        dimension_numbers=("NDHWC", "DHWIO", "NDHWC"),
        preferred_element_type=jnp.float32,
    )


def gathered_body(
    segment_input,
    inner_input,
    lengths,
    inner_gain,
    causal_weight,
    causal_bias,
    attention_gain,
    triple_weight,
    triple_bias,
    output_weight,
    output_bias,
):
    clip_count, frame_count, row_count, column_count, channels = segment_input.shape
    sections = lax.axis_size("tm")
    counts = lengths[:, 0]
    ahead = [(i, i + 1) for i in range(sections - 1)]
    prev_counts = lax.ppermute(counts, "tm", ahead)
    both = jnp.concatenate([inner_input, segment_input], axis=0)
    both_all = lax.all_gather(both, "rows", axis=2, tiled=True)
    inner_all = both_all[:clip_count]
    segment_all = both_all[clip_count:]
    wide = (counts > 1)[:, None, None, None]
    last_raw = jnp.where(wide, inner_all[:, frame_count - 1], inner_all[:, 0])
    prev_raw = lax.ppermute(inner_all, "tm", ahead)
    before_raw = lax.ppermute(last_raw, "tm", [(i, i + 2) for i in range(sections - 2)])
    own = activate(inner_all, inner_gain)
    own_part = conv3d(own, causal_weight, (2, 0))
    prev = activate(prev_raw, inner_gain)
    before = activate(before_raw, inner_gain)
    prev_wide = (prev_counts > 1)[:, None, None, None]
    carried = jnp.stack(
        [
            jnp.where(prev_wide, prev[:, frame_count - 2], before),
            jnp.where(prev_wide, prev[:, frame_count - 1], prev[:, 0]),
        ],
        axis=1,
    )
    carried_part = conv3d(carried, causal_weight, (0, frame_count))
    convolved = own_part + carried_part + causal_bias
    residual = (segment_all.astype(jnp.float32) + convolved).astype(jnp.bfloat16)
    normed = normalize(residual, attention_gain).astype(jnp.bfloat16)
    height = normed.shape[2]
    frames = clip_count * frame_count
    places = height * column_count
    flat = normed.reshape(frames * places, channels)
    packed = (
        jnp.dot(flat, triple_weight[:, channels:], preferred_element_type=jnp.float32)
        + triple_bias[channels:]
    ).reshape(frames, places, 2 * channels)
    key_vectors = packed[:, :, :channels]
    values = packed[:, :, channels:].astype(jnp.bfloat16)
    start = lax.axis_index("rows") * row_count
    mine = lax.dynamic_slice_in_dim(normed, start, row_count, axis=2)
    queries = (
        jnp.dot(
            mine.reshape(-1, channels),
            triple_weight[:, :channels],
            preferred_element_type=jnp.float32,
        )
        + triple_bias[:channels]
    ).reshape(frames, row_count * column_count, channels)
    scores = jnp.einsum(
        "nqc,nkc->nqk", queries, key_vectors, precision=lax.Precision.HIGHEST
    ) / math.sqrt(channels)
    row_max = jnp.max(scores, axis=-1, keepdims=True)
    exponent = jnp.exp(scores - row_max)
    weights = (exponent / jnp.sum(exponent, axis=-1, keepdims=True)).astype(jnp.bfloat16)
    attended = jnp.einsum(
        "nqk,nkc->nqc", weights, values, preferred_element_type=jnp.float32
    ).astype(jnp.bfloat16)
    projected = (
        jnp.dot(attended.reshape(-1, channels), output_weight, preferred_element_type=jnp.float32)
        + output_bias
    ).astype(jnp.bfloat16)
    projected = projected.reshape(clip_count, frame_count, row_count, column_count, channels)
    residual_mine = lax.dynamic_slice_in_dim(residual, start, row_count, axis=2)
    live_mask = (jnp.arange(frame_count, dtype=jnp.int32)[None, :] < counts[:, None]).astype(
        jnp.float32
    )
    summed = residual_mine.astype(jnp.float32) + projected.astype(jnp.float32)
    return (summed * live_mask[:, :, None, None, None]).astype(jnp.bfloat16)


GATHER_LIMIT = 1 << 22


def chosen_body(segment_input, inner_input, *rest):
    gathered = inner_input.size * inner_input.dtype.itemsize * lax.axis_size("rows")
    if gathered <= GATHER_LIMIT:
        return gathered_body(segment_input, inner_input, *rest)
    return body(segment_input, inner_input, *rest)


def solution(mesh):
    placed = (
        P("clips", "tm", "rows", None, None),
        P("clips", "tm", "rows", None, None),
        P("clips", "tm"),
        P(),
        P(),
        P(),
        P(),
        P(),
        P(),
        P(),
        P(),
    )
    return jax.shard_map(
        chosen_body,
        mesh=mesh,
        in_specs=placed,
        out_specs=P("clips", "tm", "rows", None, None),
        check_vma=False,
    )
```

profile of v0, /device:TPU:1, one launch (start us, length us, event | category | flops | bytes accessed | tf_op | source)
XLA Modules:
  0.0 64.8 jit_solution(6598093223761162605)
XLA Ops:
  0.0 4.6 %collective-permute-start = (s32[2]{0:T(128)}, s32[2]{0:T(128)S(1)}, u32[]{:S(2)}, u32[]{:S(2)}) collective-permute-start(s32[2]{0:T(128)} %bitcast.72), channel_id=1, source_target_pairs={{0,4},{4,8},{8,12},{1,5},{5,9},{9,13},{2,6},{6,10},{10,14},{3,7},{... | collective-permute-start | bytes 32 | tf_op jit(solution)/shard_map/ppermute | solution.py:211
  4.6 0.7 %broadcast_compare_fusion = pred[2]{0:T(512)(128)(4,1)S(1)} fusion(s32[2,1]{0,1:T(1,128)} %param.13), kind=kLoop, calls=%fused_computation.89 | loop fusion | flops 2 | bytes 10 | tf_op jit(solution)/shard_map/gt | solution.py:216
  5.3 1.0 %pad_maximum_fusion = bf16[4,2,1,32,384]{4,3,1,0,2:T(8,128)(2,1)S(1)} fusion(bf16[2,2,1,32,384]{4,3,1,0,2:T(8,128)(2,1)} %bitcast.70, bf16[2,2,1,32,384]{4,3,1,0,2:T(8,128)(2,1)} %bitcast.71), kind=kLoop, calls=%fused_computation.71 | loop fusion | flops 98304 | bytes 393216 | tf_op jit(solution)/shard_map/concatenate | solution.py:212
  6.3 17.9 %all_gather.3 = bf16[4,2,4,32,384]{4,3,1,0,2:T(8,128)(2,1)S(1)} all-gather(bf16[4,2,1,32,384]{4,3,1,0,2:T(8,128)(2,1)S(1)} %pad_maximum_fusion), channel_id=1, replica_groups=mesh['clips'=2,'tm'=4,'rows'=4] {'rows'}, dimensions={2}, use_global_device_ids=true | all-gather | bytes 983040 | tf_op jit(solution)/shard_map/all_gather | solution.py:213
  24.2 0.1 fusion.48
  24.3 0.0 copy-start.2
  24.3 1.3 %collective-permute-start.2 = (bf16[2,4,32,384]{3,2,0,1:T(8,128)(2,1)S(1)}, bf16[2,4,32,384]{3,2,0,1:T(8,128)(2,1)S(1)}, u32[]{:S(2)}, u32[]{:S(2)}) collective-permute-start(bf16[2,4,32,384]{3,2,0,1:T(8,128)(2,1)S(1)} %fusion.48), channel_id=1, source_target_pairs={{0,8},{4,12},{1,9},{5,13},{2,10},{6,14},{3,11},{7,15},{16,24},{20,... | collective-permute-start | bytes 589832 | tf_op jit(solution)/shard_map/ppermute | solution.py:219
  25.6 0.1 fusion.59
  25.8 3.9 %collective-permute-start.1 = (bf16[2,2,4,32,384]{4,3,0,2,1:T(8,128)(2,1)S(1)}, bf16[2,2,4,32,384]{4,3,0,2,1:T(8,128)(2,1)S(1)}, u32[]{:S(2)}, u32[]{:S(2)}) collective-permute-start(bf16[2,2,4,32,384]{4,3,0,2,1:T(8,128)(2,1)S(1)} %copy.107), channel_id=1, source_target_pairs={{0,4},{4,8},{8,12},{1,5},{5,9},{9,13},{2,6},{6,10},{10,14},{3,7},{... | collective-permute-start | bytes 1179656 | tf_op jit(solution)/shard_map/ppermute | solution.py:218
  29.7 0.1 compare_convert_fusion
  29.8 0.2 fusion.8
  30.0 0.1 fusion.37
  30.1 5.5 %collective-permute-done.1 = bf16[2,2,4,32,384]{4,3,0,2,1:T(8,128)(2,1)S(1)} collective-permute-done((bf16[2,2,4,32,384]{4,3,0,2,1:T(8,128)(2,1)S(1)}, bf16[2,2,4,32,384]{4,3,0,2,1:T(8,128)(2,1)S(1)}, u32[]{:S(2)}, u32[]{:S(2)}) %collective-permute-start.1) | collective-permute-done | bytes 393248 | tf_op jit(solution)/shard_map/ppermute | solution.py:218
  35.6 0.2 fusion.16
  35.8 0.5 fusion.45
  36.3 0.3 copy.110
  36.7 0.4 pad.clone
  37.0 0.1 slice.57
  37.1 0.6 fusion.30
  37.7 0.1 slice_select_fusion
  37.8 0.2 fusion.51
  38.1 0.0 copy-start.4
  38.1 0.3 copy.111
  38.5 0.4 pad.2.clone
  38.8 0.1 slice.62
  39.0 0.0 slice-start
  39.0 0.6 fusion.31
  39.6 0.0 slice-start.1
  39.6 0.0 copy-start.5
  39.6 13.2 %convolution_select_fusion = f32[2,4,16,5,384]{4,2,3,1,0:T(8,128)S(1)} fusion(bf16[3,3,3,384,384]{4,3,2,1,0:T(8,128)(2,1)} %param.15, bf16[2,4,2,8,7,384]{5,2,4,3,1,0:T(2,128)(2,1)S(1)} %fusion.31, pred[16,5]{0,1:T(8,128)(4,1)S(1)} %copy-done.4), kind=kOutput, calls=%fused_computation.5 | convolution fusion | flops 2123612160 | bytes 9633872 | tf_op jit(solution)/shard_map/conv_general_dilated | solution.py:184
  52.8 7.0 %fusion.4 = f32[2,4,16,5,384]{4,2,3,1,0:T(8,128)S(1)} fusion(f32[2,4,16,5,384]{4,2,3,1,0:T(8,128)S(1)} %convolution_select_fusion, bf16[3,3,3,384,384]{4,3,2,1,0:T(8,128)(2,1)S(1)} %bitcast.57, bf16[2,4,2,8,7,384]{5,2,4,3,1,0:T(2,128)(2,1)S(1)} %fusion.30, f32[384]{0:T(512)S(1)} %copy-done.5, pred[16,5]{0,1:T(8,128)(4,1)S(1)} %copy-done.4), kind=kOutput, calls=%fused_computation.8 | convolution fusion | flops 2124103680 | bytes 10618448 | tf_op jit(solution)/shard_map/conv_general_dilated | solution.py:184
  59.9 0.4 copy.101
  60.2 0.0 copy-start.6
  60.3 0.1 slice.63
  60.4 0.0 slice-start.2
  60.4 0.2 fusion.24
  60.6 0.3 copy-done.6
  60.9 0.2 fusion.26
  61.1 0.4 copy-done.1
  61.5 0.0 slice-done.2
  61.5 0.2 convolution_add_fusion.2
  61.7 0.6 convolution_add_fusion
  62.3 0.9 %convolution_multiply_fusion = f32[4,32,128]{2,1,0:T(8,128)S(1)} fusion(f32[4,32,384]{2,1,0:T(8,128)S(1)} %bitcast.66, f32[4,128,768]{2,1,0:T(8,128)S(1)} %bitcast.58), kind=kOutput, calls=%fused_computation.15 | convolution fusion | flops 75513856 | bytes 1048576 | tf_op jit(solution)/shard_map/nqc,nkc->nqk/dot_general | solution.py:256
  63.3 0.2 fusion.60
  63.5 0.3 convolution_convert_fusion
  63.8 0.0 copy-done
  63.8 0.2 fusion.5
  64.0 0.7 %fusion.50 = bf16[2,2,1,32,384]{4,3,2,1,0:T(8,128)(2,1)} fusion(bf16[2,2,1,32,384]{4,3,2,1,0:T(8,128)(2,1)S(1)} %bitcast.69, f32[2,2]{1,0:T(2,128)S(1)} %compare_convert_fusion, bf16[2,2,4,32,384]{4,3,2,1,0:T(8,128)(2,1)S(1)} %get-tuple-element.6, s32[]{:T(128)S(6)} %select_n.18), kind=kLoop, calls=%fused_computation.74 | loop fusion | flops 245760 | bytes 294932 | tf_op jit(solution)/shard_map/convert_element_type | solution.py:275
  (27 shorter events, 0.2 us)
Async XLA Ops:
  0.0 63.8 %copy-start = (bf16[384,384]{1,0:T(8,128)(2,1)S(1)}, bf16[384,384]{1,0:T(8,128)(2,1)}, u32[]{:S(2)}) copy-start(bf16[384,384]{1,0:T(8,128)(2,1)} %param.20) | copy-start | bytes 884740
  0.0 30.0 %collective-permute-start = (s32[2]{0:T(128)}, s32[2]{0:T(128)S(1)}, u32[]{:S(2)}, u32[]{:S(2)}) collective-permute-start(s32[2]{0:T(128)} %bitcast.72), channel_id=1, source_target_pairs={{0,4},{4,8},{8,12},{1,5},{5,9},{9,13},{2,6},{6,10},{10,14},{3,7},{... | collective-permute-start | bytes 32 | tf_op jit(solution)/shard_map/ppermute | solution.py:211
  24.2 5.5 %copy-start.8 = (s32[2,1]{0,1:T(1,128)S(1)}, s32[2,1]{0,1:T(1,128)}, u32[]{:S(2)}) copy-start(s32[2,1]{0,1:T(1,128)} %param.13) | copy-start | bytes 28
  24.2 5.6 %copy-start.3 = (f32[1152]{0:T(1024)S(1)}, f32[1152]{0:T(1024)}, u32[]{:S(2)}) copy-start(f32[1152]{0:T(1024)} %param.19) | copy-start | bytes 13828
  24.3 11.5 %copy-start.2 = (f32[384]{0:T(512)S(1)}, f32[384]{0:T(512)}, u32[]{:S(2)}) copy-start(f32[384]{0:T(512)} %param.14) | copy-start | bytes 4612
  24.3 5.7 %collective-permute-start.2 = (bf16[2,4,32,384]{3,2,0,1:T(8,128)(2,1)S(1)}, bf16[2,4,32,384]{3,2,0,1:T(8,128)(2,1)S(1)}, u32[]{:S(2)}, u32[]{:S(2)}) collective-permute-start(bf16[2,4,32,384]{3,2,0,1:T(8,128)(2,1)S(1)} %fusion.48), channel_id=1, source_target_pairs={{0,8},{4,12},{1,9},{5,13},{2,10},{6,14},{3,11},{7,15},{16,24},{20,... | collective-permute-start | bytes 589832 | tf_op jit(solution)/shard_map/ppermute | solution.py:219
  25.8 9.8 %collective-permute-start.1 = (bf16[2,2,4,32,384]{4,3,0,2,1:T(8,128)(2,1)S(1)}, bf16[2,2,4,32,384]{4,3,0,2,1:T(8,128)(2,1)S(1)}, u32[]{:S(2)}, u32[]{:S(2)}) collective-permute-start(bf16[2,2,4,32,384]{4,3,0,2,1:T(8,128)(2,1)S(1)} %copy.107), channel_id=1, source_target_pairs={{0,4},{4,8},{8,12},{1,5},{5,9},{9,13},{2,6},{6,10},{10,14},{3,7},{... | collective-permute-start | bytes 1179656 | tf_op jit(solution)/shard_map/ppermute | solution.py:218
  38.1 1.4 %copy-start.4 = (pred[16,5]{0,1:T(8,128)(4,1)S(1)}, pred[16,5]{0,1:T(8,128)(4,1)}, u32[]{:S(2)}) copy-start(pred[16,5]{0,1:T(8,128)(4,1)} %constant.44) | copy-start | bytes 244
  39.0 13.8 %slice-start = ((s8[7962624]{0:T(1024)(128)(4,1)}), s8[4194304]{0:T(1024)(128)(4,1)S(1)}, s32[]{:S(2)}) async-start(s8[7962624]{0:T(1024)(128)(4,1)} %bitcast.56), calls=%async_computation | async-start | bytes 8388608
  39.6 13.2 %slice-start.1 = ((s8[7962624]{0:T(1024)(128)(4,1)}), s8[3768320]{0:T(1024)(128)(4,1)S(1)}, s32[]{:S(2)}) async-start(s8[7962624]{0:T(1024)(128)(4,1)} %bitcast.56), calls=%async_computation.1 | async-start | bytes 7536640
  39.6 13.2 %copy-start.5 = (f32[384]{0:T(512)S(1)}, f32[384]{0:T(512)}, u32[]{:S(2)}) copy-start(f32[384]{0:T(512)} %param.16) | copy-start | bytes 4612
  60.2 0.7 %copy-start.6 = (f32[384]{0:T(512)S(1)}, f32[384]{0:T(512)}, u32[]{:S(2)}) copy-start(f32[384]{0:T(512)} %param.17) | copy-start | bytes 4612
  60.3 1.2 %copy-start.1 = (bf16[384,1152]{1,0:T(8,128)(2,1)S(1)}, bf16[384,1152]{1,0:T(8,128)(2,1)}, u32[]{:S(2)}) copy-start(bf16[384,1152]{1,0:T(8,128)(2,1)} %param.18) | copy-start | bytes 2654212
  60.4 1.2 %slice-start.2 = ((f32[1152]{0:T(1024)}), f32[384]{0:T(512)S(1)}, s32[]{:S(2)}) async-start(f32[1152]{0:T(1024)} %param.19), calls=%async_computation.2 | async-start | bytes 4096 | tf_op jit(solution)/shard_map/slice | solution.py:254
  62.3 1.5 %copy-start.7 = (f32[384]{0:T(512)S(1)}, f32[384]{0:T(512)}, u32[]{:S(2)}) copy-start(f32[384]{0:T(512)} %param.21) | copy-start | bytes 4612
where the time goes:
time: 65 us; the launch traced here: 64.8 us
  matrix products  22.4 us (34%)
  blocking collectives  17.9 us (28%)
  starting transfers between devices  9.81 us (15%)
  other arithmetic  5.62 us (9%)
  waiting for transfers between devices  5.46 us (8%)
  local copies, waits for them, and re-layouts  3.06 us (5%)
    conv_general_dilated x2, matrix products, conv3d(): lax.conv_general_dilated(frames, causal_weight, window_strides=(1, 1, 1),...  20.2 us
    all_gather x1, blocking collectives, gathered_body(): both_all = lax.all_gather(both, 'rows', axis=2, tiled=True)  17.9 us
    ppermute x1, waiting for transfers between devices, gathered_body(): prev_raw = lax.ppermute(inner_all, 'tm', ahead)  5.46 us
    ppermute x1, starting transfers between devices, gathered_body(): prev_counts = lax.ppermute(counts, 'tm', ahead)  4.63 us
    ppermute x1, starting transfers between devices, gathered_body(): prev_raw = lax.ppermute(inner_all, 'tm', ahead)  3.88 us
    unnamed x25, local copies, waits for them, and re-layouts  1.5 us
    ppermute x1, starting transfers between devices, gathered_body(): lax.ppermute(last_raw, 'tm', [(i, i + 2) for i in range(sections - 2)])  1.3 us
  transfers between devices with their start and end apart: 3, of which 1 were waited for; matrix products, arithmetic and copies ran while one was open for 3% of the time, Pallas kernels for 0%

commit v1 on v0

--- a/solution.py
+++ b/solution.py
@@ -210,7 +210,12 @@
     ahead = [(i, i + 1) for i in range(sections - 1)]
     prev_counts = lax.ppermute(counts, "tm", ahead)
     both = jnp.concatenate([inner_input, segment_input], axis=0)
-    both_all = lax.all_gather(both, "rows", axis=2, tiled=True)
+    ring = [both]
+    for hop in range(3):
+        ring.append(lax.ppermute(ring[-1], "rows", [(dev, (dev + 1) % 4) for dev in range(4)]))
+    both_all = jnp.roll(
+        jnp.concatenate(ring[::-1], axis=2), (lax.axis_index("rows") + 1) * ring[0].shape[2], axis=2
+    )
     inner_all = both_all[:clip_count]
     segment_all = both_all[clip_count:]
     wide = (counts > 1)[:, None, None, None]

time: 65 us -> 62.8 us (0.966)
  blocking collectives: 17.9 us -> 0 us
  waiting for transfers between devices: 5.46 us -> 21.3 us
  matrix products: 22.4 us -> 16.5 us
  starting transfers between devices: 9.81 us -> 13.8 us
  local copies, waits for them, and re-layouts: 3.06 us -> 4.09 us
  other arithmetic: 5.62 us -> 6.35 us
    all_gather x1 -> x0, blocking collectives: 17.9 us -> none  [gathered_body(): both_all = lax.all_gather(both, 'rows', axis=2, tiled=True)]
    ppermute x0 -> x3, waiting for transfers between devices: none -> 13.8 us  [gathered_body(): lax.ppermute(ring[-1], 'rows', [(dev, (dev + 1) % 4) for dev in range(4)])]
    ppermute x1, waiting for transfers between devices: 0.01 us -> 7.49 us  [gathered_body(): lax.ppermute(last_raw, 'tm', [(i, i + 2) for i in range(sections - 2)])]
    conv_general_dilated x2, matrix products: 20.2 us -> 14.2 us  [conv3d(): lax.conv_general_dilated(frames, causal_weight, window_strides=(1, 1, 1),...]
    ppermute x1, waiting for transfers between devices: 5.46 us -> 0.01 us  [gathered_body(): prev_raw = lax.ppermute(inner_all, 'tm', ahead)]
    ppermute x1, starting transfers between devices: 3.88 us -> 6.32 us  [gathered_body(): prev_raw = lax.ppermute(inner_all, 'tm', ahead)]
    ppermute x0 -> x3, starting transfers between devices: none -> 2.22 us  [gathered_body(): lax.ppermute(ring[-1], 'rows', [(dev, (dev + 1) % 4) for dev in range(4)])]
    slice x1, local copies, waits for them, and re-layouts: 0.01 us -> 0.7 us  [gathered_body(): triple_bias[channels:]]
  transfers between devices with their start and end apart: 3 -> 6, of which waited for: 1 -> 4; matrix products, arithmetic and copies ran while one was open for 3% -> 4% of each run, Pallas kernels for 0% -> 0%
where the time goes in v1:
time: 62.8 us; the launch traced here: 62.5 us
  waiting for transfers between devices  21.3 us (34%)
  matrix products  16.5 us (26%)
  starting transfers between devices  13.8 us (22%)
  other arithmetic  6.35 us (10%)
  local copies, waits for them, and re-layouts  4.09 us (7%)
    conv_general_dilated x2, matrix products, conv3d(): lax.conv_general_dilated(frames, causal_weight, window_strides=(1, 1, 1),...  14.2 us
    ppermute x3, waiting for transfers between devices, gathered_body(): lax.ppermute(ring[-1], 'rows', [(dev, (dev + 1) % 4) for dev in range(4)])  13.8 us
    ppermute x1, waiting for transfers between devices, gathered_body(): lax.ppermute(last_raw, 'tm', [(i, i + 2) for i in range(sections - 2)])  7.49 us
    ppermute x1, starting transfers between devices, gathered_body(): prev_raw = lax.ppermute(inner_all, 'tm', ahead)  6.32 us
    ppermute x1, starting transfers between devices, gathered_body(): prev_counts = lax.ppermute(counts, 'tm', ahead)  3.95 us
    ppermute x3, starting transfers between devices, gathered_body(): lax.ppermute(ring[-1], 'rows', [(dev, (dev + 1) % 4) for dev in range(4)])  2.22 us
    unnamed x34, local copies, waits for them, and re-layouts  1.89 us
    ppermute x1, starting transfers between devices, gathered_body(): lax.ppermute(last_raw, 'tm', [(i, i + 2) for i in range(sections - 2)])  1.3 us
  transfers between devices with their start and end apart: 6, of which 4 were waited for; matrix products, arithmetic and copies ran while one was open for 4% of the time, Pallas kernels for 0%

profile of v1, /device:TPU:1, one launch (start us, length us, event | category | flops | bytes accessed | tf_op | source)
XLA Modules:
  0.0 62.5 jit_solution(10266855296763329473)
XLA Ops:
  0.0 1.0 %pad_maximum_fusion = bf16[4,2,1,32,384]{4,3,2,1,0:T(8,128)(2,1)S(1)} fusion(bf16[2,2,1,32,384]{4,3,2,1,0:T(8,128)(2,1)} %param.11, bf16[2,2,1,32,384]{4,3,2,1,0:T(8,128)(2,1)} %param.12), kind=kLoop, calls=%fused_computation.71 | loop fusion | flops 98304 | bytes 393216 | tf_op jit(solution)/shard_map/concatenate | solution.py:212
  1.0 2.2 %collective-permute-start = (bf16[4,2,1,32,384]{4,3,2,1,0:T(8,128)(2,1)S(1)}, bf16[4,2,1,32,384]{4,3,2,1,0:T(8,128)(2,1)S(1)}, u32[]{:S(2)}, u32[]{:S(2)}) collective-permute-start(bf16[4,2,1,32,384]{4,3,2,1,0:T(8,128)(2,1)S(1)} %pad_maximum_fusion), channel_id=1, source_target_pairs={{0,1},{1,2},{2,3},{3,0},{4,5},{5,6},{6,7},{7,4},{8,9},{9,10},{10,1... | collective-permute-start | bytes 589832 | tf_op jit(solution)/shard_map/ppermute | solution.py:215
  3.2 4.0 %collective-permute-start.3 = (s32[2]{0:T(128)}, s32[2]{0:T(128)S(1)}, u32[]{:S(2)}, u32[]{:S(2)}) collective-permute-start(s32[2]{0:T(128)} %bitcast.68), channel_id=1, source_target_pairs={{0,4},{4,8},{8,12},{1,5},{5,9},{9,13},{2,6},{6,10},{10,14},{3,7},{... | collective-permute-start | bytes 32 | tf_op jit(solution)/shard_map/ppermute | solution.py:211
  7.2 0.7 %slice.49 = f32[768]{0:T(1024)S(1)} slice(f32[1152]{0:T(1024)} %param.19), slice={[384:1152]} | slice | bytes 6144 | tf_op jit(solution)/shard_map/slice | solution.py:247
  7.9 0.7 %compare_convert_fusion = f32[2,2]{1,0:T(2,128)S(1)} fusion(s32[2]{0:T(128)} %bitcast.69), kind=kLoop, calls=%fused_computation.94 | loop fusion | flops 8 | bytes 24 | tf_op jit(solution)/shard_map/convert_element_type | solution.py:276
  8.6 1.3 %collective-permute-done = bf16[4,2,1,32,384]{4,3,2,1,0:T(8,128)(2,1)S(1)} collective-permute-done((bf16[4,2,1,32,384]{4,3,2,1,0:T(8,128)(2,1)S(1)}, bf16[4,2,1,32,384]{4,3,2,1,0:T(8,128)(2,1)S(1)}, u32[]{:S(2)}, u32[]{:S(2)}) %collective-permute-start) | collective-permute-done | bytes 196640 | tf_op jit(solution)/shard_map/ppermute | solution.py:215
  9.9 0.0 collective-permute-start.1
  9.9 0.7 %broadcast_compare_fusion = pred[2]{0:T(512)(128)(4,1)S(1)} fusion(s32[2,1]{0,1:T(1,128)} %param.13), kind=kLoop, calls=%fused_computation.98 | loop fusion | flops 2 | bytes 10 | tf_op jit(solution)/shard_map/gt | solution.py:221
  10.6 6.3 %collective-permute-done.1 = bf16[4,2,1,32,384]{4,3,2,1,0:T(8,128)(2,1)S(1)} collective-permute-done((bf16[4,2,1,32,384]{4,3,2,1,0:T(8,128)(2,1)S(1)}, bf16[4,2,1,32,384]{4,3,2,1,0:T(8,128)(2,1)S(1)}, u32[]{:S(2)}, u32[]{:S(2)}) %collective-permute-start.1) | collective-permute-done | bytes 196640 | tf_op jit(solution)/shard_map/ppermute | solution.py:215
  16.9 6.3 %collective-permute-done.2 = bf16[4,2,1,32,384]{4,3,2,1,0:T(8,128)(2,1)S(1)} collective-permute-done((bf16[4,2,1,32,384]{4,3,2,1,0:T(8,128)(2,1)S(1)}, bf16[4,2,1,32,384]{4,3,2,1,0:T(8,128)(2,1)S(1)}, u32[]{:S(2)}, u32[]{:S(2)}) %collective-permute-start.2) | collective-permute-done | bytes 196640 | tf_op jit(solution)/shard_map/ppermute | solution.py:215
  23.3 0.0 slice-start
  23.5 0.2 fusion.8
  23.8 6.3 %collective-permute-start.4 = (bf16[2,2,4,32,384]{4,3,2,0,1:T(8,128)(2,1)S(1)}, bf16[2,2,4,32,384]{4,3,2,0,1:T(8,128)(2,1)S(1)}, u32[]{:S(2)}, u32[]{:S(2)}) collective-permute-start(bf16[2,2,4,32,384]{4,3,2,0,1:T(8,128)(2,1)S(1)} %copy.70), channel_id=1, source_target_pairs={{0,4},{4,8},{8,12},{1,5},{5,9},{9,13},{2,6},{6,10},{10,14},{3,7},{... | collective-permute-start | bytes 1179656 | tf_op jit(solution)/shard_map/ppermute | solution.py:223
  30.1 0.1 fusion.48
  30.2 1.3 %collective-permute-start.5 = (bf16[2,4,32,384]{3,2,1,0:T(8,128)(2,1)S(1)}, bf16[2,4,32,384]{3,2,1,0:T(8,128)(2,1)S(1)}, u32[]{:S(2)}, u32[]{:S(2)}) collective-permute-start(bf16[2,4,32,384]{3,2,1,0:T(8,128)(2,1)S(1)} %fusion.48), channel_id=1, source_target_pairs={{0,8},{4,12},{1,9},{5,13},{2,10},{6,14},{3,11},{7,15},{16,24},{20,... | collective-permute-start | bytes 589832 | tf_op jit(solution)/shard_map/ppermute | solution.py:224
  31.6 7.5 %collective-permute-done.5 = bf16[2,4,32,384]{3,2,1,0:T(8,128)(2,1)S(1)} collective-permute-done((bf16[2,4,32,384]{3,2,1,0:T(8,128)(2,1)S(1)}, bf16[2,4,32,384]{3,2,1,0:T(8,128)(2,1)S(1)}, u32[]{:S(2)}, u32[]{:S(2)}) %collective-permute-start.5) | collective-permute-done | bytes 196640 | tf_op jit(solution)/shard_map/ppermute | solution.py:224
  39.1 0.1 fusion.37
  39.2 0.2 fusion.16
  39.4 0.5 fusion.45
  39.9 0.1 slice_select_fusion
  40.0 0.0 slice-start.1
  40.0 0.2 fusion.51
  40.3 0.4 copy.74
  40.7 0.4 pad.2.clone
  41.1 0.1 slice.58
  41.2 0.6 fusion.31
  41.8 0.0 copy-start.5
  41.8 0.4 copy.73
  42.2 0.4 pad.clone
  42.6 0.1 slice.55
  42.7 0.6 fusion.30
  43.4 7.0 %convolution_select_fusion = f32[2,4,16,5,384]{4,2,3,1,0:T(8,128)S(1)} fusion(bf16[3,3,3,384,384]{4,3,2,1,0:T(8,128)(2,1)S(1)} %bitcast.55, bf16[2,4,2,8,7,384]{5,2,4,3,1,0:T(2,128)(2,1)S(1)} %fusion.31, pred[16,5]{0,1:T(8,128)(4,1)S(1)} %copy-done.5), kind=kOutput, calls=%fused_computation.5 | convolution fusion | flops 2123612160 | bytes 9633872 | tf_op jit(solution)/shard_map/conv_general_dilated | solution.py:184
  50.4 7.2 %fusion.4 = f32[2,4,16,5,384]{4,2,3,1,0:T(8,128)S(1)} fusion(f32[2,4,16,5,384]{4,2,3,1,0:T(8,128)S(1)} %convolution_select_fusion, bf16[3,3,3,384,384]{4,3,2,1,0:T(8,128)(2,1)S(1)} %bitcast.55, bf16[2,4,2,8,7,384]{5,2,4,3,1,0:T(2,128)(2,1)S(1)} %fusion.30, f32[384]{0:T(512)S(1)} %copy-done.6, pred[16,5]{0,1:T(8,128)(4,1)S(1)} %copy-done.5), kind=kOutput, calls=%fused_computation.8 | convolution fusion | flops 2124103680 | bytes 10618448 | tf_op jit(solution)/shard_map/conv_general_dilated | solution.py:184
  57.6 0.4 copy.66
  58.0 0.1 slice.59
  58.1 0.2 fusion.24
  58.3 0.4 copy-done.7
  58.7 0.2 fusion.26
  58.9 0.0 slice-start.2
  58.9 0.4 copy-done.1
  59.3 0.6 convolution_add_fusion
  59.9 0.2 convolution_add_fusion.2
  60.1 1.0 %convolution_multiply_fusion = f32[4,32,128]{2,1,0:T(8,128)S(1)} fusion(f32[4,32,384]{2,1,0:T(8,128)S(1)} %bitcast.64, f32[4,128,768]{2,1,0:T(8,128)S(1)} %bitcast.56), kind=kOutput, calls=%fused_computation.15 | convolution fusion | flops 75513856 | bytes 1048576 | tf_op jit(solution)/shard_map/nqc,nkc->nqk/dot_general | solution.py:261
  61.1 0.2 fusion.57
  61.2 0.3 convolution_convert_fusion
  61.6 0.0 copy-done
  61.6 0.2 fusion.5
  61.8 0.7 %fusion.50 = bf16[2,2,1,32,384]{4,3,2,1,0:T(8,128)(2,1)} fusion(bf16[2,2,1,32,384]{4,3,2,1,0:T(8,128)(2,1)S(1)} %bitcast.67, f32[2,2]{1,0:T(2,128)S(1)} %compare_convert_fusion, bf16[2,2,4,32,384]{4,3,2,1,0:T(8,128)(2,1)S(1)} %get-tuple-element.6, s32[]{:T(128)S(6)} %select_n.33), kind=kLoop, calls=%fused_computation.74 | loop fusion | flops 245760 | bytes 294932 | tf_op jit(solution)/shard_map/convert_element_type | solution.py:280
  (39 shorter events, 0.5 us)
Async XLA Ops:
  0.0 61.6 %copy-start = (bf16[384,384]{1,0:T(8,128)(2,1)S(1)}, bf16[384,384]{1,0:T(8,128)(2,1)}, u32[]{:S(2)}) copy-start(bf16[384,384]{1,0:T(8,128)(2,1)} %param.20) | copy-start | bytes 884740
  0.0 23.3 %copy-start.3 = (bf16[2,2,1,32,384]{4,3,2,1,0:T(8,128)(2,1)S(1)}, bf16[2,2,1,32,384]{4,3,2,1,0:T(8,128)(2,1)}, u32[]{:S(2)}) copy-start(bf16[2,2,1,32,384]{4,3,2,1,0:T(8,128)(2,1)} %param.11) | copy-start | bytes 294916
  0.0 23.3 %copy-start.2 = (bf16[2,2,1,32,384]{4,3,2,1,0:T(8,128)(2,1)S(1)}, bf16[2,2,1,32,384]{4,3,2,1,0:T(8,128)(2,1)}, u32[]{:S(2)}) copy-start(bf16[2,2,1,32,384]{4,3,2,1,0:T(8,128)(2,1)} %param.12) | copy-start | bytes 294916
  1.0 8.8 %collective-permute-start = (bf16[4,2,1,32,384]{4,3,2,1,0:T(8,128)(2,1)S(1)}, bf16[4,2,1,32,384]{4,3,2,1,0:T(8,128)(2,1)S(1)}, u32[]{:S(2)}, u32[]{:S(2)}) collective-permute-start(bf16[4,2,1,32,384]{4,3,2,1,0:T(8,128)(2,1)S(1)} %pad_maximum_fusion), channel_id=1, source_target_pairs={{0,1},{1,2},{2,3},{3,0},{4,5},{5,6},{6,7},{7,4},{8,9},{9,10},{10,1... | collective-permute-start | bytes 589832 | tf_op jit(solution)/shard_map/ppermute | solution.py:215
  3.2 13.6 %collective-permute-start.3 = (s32[2]{0:T(128)}, s32[2]{0:T(128)S(1)}, u32[]{:S(2)}, u32[]{:S(2)}) collective-permute-start(s32[2]{0:T(128)} %bitcast.68), channel_id=1, source_target_pairs={{0,4},{4,8},{8,12},{1,5},{5,9},{9,13},{2,6},{6,10},{10,14},{3,7},{... | collective-permute-start | bytes 32 | tf_op jit(solution)/shard_map/ppermute | solution.py:211
  9.9 7.0 %collective-permute-start.1 = (bf16[4,2,1,32,384]{4,3,2,1,0:T(8,128)(2,1)S(1)}, bf16[4,2,1,32,384]{4,3,2,1,0:T(8,128)(2,1)S(1)}, u32[]{:S(2)}, u32[]{:S(2)}) collective-permute-start(bf16[4,2,1,32,384]{4,3,2,1,0:T(8,128)(2,1)S(1)} %collective-permute-done), channel_id=1, source_target_pairs={{0,1},{1,2},{2,3},{3,0},{4,5},{5,6},{6,7},{7,4},{8,9},{9,10},{10,1... | collective-permute-start | bytes 589832 | tf_op jit(solution)/shard_map/ppermute | solution.py:215
  16.8 6.3 %collective-permute-start.2 = (bf16[4,2,1,32,384]{4,3,2,1,0:T(8,128)(2,1)S(1)}, bf16[4,2,1,32,384]{4,3,2,1,0:T(8,128)(2,1)S(1)}, u32[]{:S(2)}, u32[]{:S(2)}) collective-permute-start(bf16[4,2,1,32,384]{4,3,2,1,0:T(8,128)(2,1)S(1)} %collective-permute-done.1), channel_id=1, source_target_pairs={{0,1},{1,2},{2,3},{3,0},{4,5},{5,6},{6,7},{7,4},{8,9},{9,10},{10,1... | collective-permute-start | bytes 589832 | tf_op jit(solution)/shard_map/ppermute | solution.py:215
  23.3 20.0 %slice-start = ((s8[7962624]{0:T(1024)(128)(4,1)}), s8[4194304]{0:T(1024)(128)(4,1)S(1)}, s32[]{:S(2)}) async-start(s8[7962624]{0:T(1024)(128)(4,1)} %bitcast.54), calls=%async_computation | async-start | bytes 8388608
  23.5 15.8 %copy-start.4 = (f32[384]{0:T(512)S(1)}, f32[384]{0:T(512)}, u32[]{:S(2)}) copy-start(f32[384]{0:T(512)} %param.14) | copy-start | bytes 4612
  23.8 15.4 %collective-permute-start.4 = (bf16[2,2,4,32,384]{4,3,2,0,1:T(8,128)(2,1)S(1)}, bf16[2,2,4,32,384]{4,3,2,0,1:T(8,128)(2,1)S(1)}, u32[]{:S(2)}, u32[]{:S(2)}) collective-permute-start(bf16[2,2,4,32,384]{4,3,2,0,1:T(8,128)(2,1)S(1)} %copy.70), channel_id=1, source_target_pairs={{0,4},{4,8},{8,12},{1,5},{5,9},{9,13},{2,6},{6,10},{10,14},{3,7},{... | collective-permute-start | bytes 1179656 | tf_op jit(solution)/shard_map/ppermute | solution.py:223
  30.2 8.8 %collective-permute-start.5 = (bf16[2,4,32,384]{3,2,1,0:T(8,128)(2,1)S(1)}, bf16[2,4,32,384]{3,2,1,0:T(8,128)(2,1)S(1)}, u32[]{:S(2)}, u32[]{:S(2)}) collective-permute-start(bf16[2,4,32,384]{3,2,1,0:T(8,128)(2,1)S(1)} %fusion.48), channel_id=1, source_target_pairs={{0,8},{4,12},{1,9},{5,13},{2,10},{6,14},{3,11},{7,15},{16,24},{20,... | collective-permute-start | bytes 589832 | tf_op jit(solution)/shard_map/ppermute | solution.py:224
  40.0 3.3 %slice-start.1 = ((s8[7962624]{0:T(1024)(128)(4,1)}), s8[3768320]{0:T(1024)(128)(4,1)S(1)}, s32[]{:S(2)}) async-start(s8[7962624]{0:T(1024)(128)(4,1)} %bitcast.54), calls=%async_computation.1 | async-start | bytes 7536640
  41.8 1.5 %copy-start.5 = (pred[16,5]{0,1:T(8,128)(4,1)S(1)}, pred[16,5]{0,1:T(8,128)(4,1)}, u32[]{:S(2)}) copy-start(pred[16,5]{0,1:T(8,128)(4,1)} %constant.65) | copy-start | bytes 244
  43.4 7.0 %copy-start.6 = (f32[384]{0:T(512)S(1)}, f32[384]{0:T(512)}, u32[]{:S(2)}) copy-start(f32[384]{0:T(512)} %param.16) | copy-start | bytes 4612
  58.0 0.7 %copy-start.7 = (f32[384]{0:T(512)S(1)}, f32[384]{0:T(512)}, u32[]{:S(2)}) copy-start(f32[384]{0:T(512)} %param.17) | copy-start | bytes 4612
  58.1 1.2 %copy-start.1 = (bf16[384,1152]{1,0:T(8,128)(2,1)S(1)}, bf16[384,1152]{1,0:T(8,128)(2,1)}, u32[]{:S(2)}) copy-start(bf16[384,1152]{1,0:T(8,128)(2,1)} %param.18) | copy-start | bytes 2654212
  58.9 1.0 %slice-start.2 = ((f32[1152]{0:T(1024)}), f32[384]{0:T(512)S(1)}, s32[]{:S(2)}) async-start(f32[1152]{0:T(1024)} %param.19), calls=%async_computation.2 | async-start | bytes 4096 | tf_op jit(solution)/shard_map/slice | solution.py:259
  59.9 1.7 %copy-start.8 = (f32[384]{0:T(512)S(1)}, f32[384]{0:T(512)}, u32[]{:S(2)}) copy-start(f32[384]{0:T(512)} %param.21) | copy-start | bytes 4612
